TPU v7x, 32 devices: a whole 2x2x4 slice. The times are simulated.
32 devices in a mesh: sky: 8 (over z, x), visit: 4 (over y, core).
Axes of the slice: x: 2, y: 2, z: 4, core: 2. Of those that a mesh axis runs over, the one named last changes fastest.
Arguments:
- tile_image: bfloat16 [4, 256, 128, 128], P('visit', 'sky'), may hold values from -1.1953125 to 1.1953125
- tile_variance: bfloat16 [4, 256, 128, 128], P('visit', 'sky'), may hold values from 0.099609375 to 10
- match_coeffs: bfloat16 [4, 256, 9], P('visit', 'sky'), may hold values from 0.25 to 9
- tile_patch: int32 [4, 256, 1], P('visit', 'sky'), may hold values from 0 to 7; in each aligned block of 32 rows (0 to 31, 32 to 63, ..., all dimensions but the last counted through in order) at most 8 rows name the same one
- tile_offset: int32 [4, 256], P('visit', 'sky'), may hold values from 0 to 63
- row_taps: bfloat16 [9, 41], replicated, may hold values from -1.1953125 to 1.1953125
- col_taps: bfloat16 [9, 41], replicated, may hold values from -1.1953125 to 1.1953125
Outputs:
- coadd_image: float32 [8192, 1024], P('sky', 'visit')
- coadd_variance: float32 [8192, 1024], P('sky', 'visit')
- coadd_psf: float32 [8, 41, 41], P('sky')
Inputs may be any that keep to these rules, and one draw needn't show every extreme that they name: `tile_patch`: among the 32 tiles of one device, at most 8 intersect any one patch.
All inputs are finite; a program needn't handle non-finite values.
Results may differ from a plain program's by a relative error of at most 0.0029.
Values may be sent and summed in bfloat16 or wider, within the bound.
No kernel may reach another device: no remote copies, remote signals or barrier semaphores. Data moves between devices by JAX's collectives and lax.ppermute only.
A program may use at most 64 MiB of HBM per device.

v0:
```python
import jax
import jax.numpy as jnp
from jax import lax
from jax.sharding import PartitionSpec as P

GRID = 8
BASIS = 9


weight_floor = 0.5


def band_table(taps, tile):
    span = taps.shape[1]
    offset = jnp.arange(tile)[:, None] - jnp.arange(tile)[None, :] + (span - 1) // 2
    select = (offset[None, :, :] == jnp.arange(span)[:, None, None]).astype(jnp.float32)
    return jnp.einsum("kt,tij->kij", taps.astype(jnp.float32), select).astype(jnp.bfloat16)


def match_tiles(images, coeffs, row_side, col_side):
    tile = images.shape[1]

    def single(pair):
        image, coeff = pair
        first = jnp.dot(image, row_side, preferred_element_type=jnp.float32).reshape(
            tile, BASIS, tile
        )
        scaled = (first * coeff.astype(jnp.float32)[None, :, None]).astype(jnp.bfloat16)
        return jnp.dot(
            col_side, scaled.reshape(tile * BASIS, tile), preferred_element_type=jnp.float32
        )

    return lax.map(single, (images, coeffs), batch_size=16)


def weigh(images, variance, coeffs, valid, row_side, col_side):
    matched = match_tiles(images, coeffs, row_side, col_side)
    var_wide = variance.astype(jnp.float32)
    mean_var = jnp.mean(var_wide, axis=(1, 2))
    weight = jnp.where(valid, 1.0 / jnp.where(valid, mean_var, 1.0), 0.0)
    return (
        weight[:, None, None] * matched,
        (weight * weight)[:, None, None] * var_wide,
        weight,
        weight[:, None] * coeffs.astype(jnp.float32),
    )


def shards(tile_image, tile_variance, match_coeffs, tile_patch, tile_offset, row_taps, col_taps):
    n_sky = lax.axis_size("sky")
    images = tile_image[0]
    variance = tile_variance[0]
    coeffs = match_coeffs[0]
    count = images.shape[0]
    tile = images.shape[1]
    held_most = max(2, 2 * count // n_sky)
    patch_side = tile * GRID
    dest = tile_patch[0, :, 0]
    offsets = tile_offset[0]
    band_row = band_table(row_taps, tile)
    band_col = band_table(col_taps, tile)
    row_side = band_row.transpose(1, 0, 2).reshape(tile, BASIS * tile)
    col_side = band_col.transpose(2, 1, 0).reshape(tile, tile * BASIS)
    order = jnp.arange(count)
    earlier = (dest[:, None] == dest[None, :]) & (order[None, :] < order[:, None])
    rank = jnp.sum(earlier.astype(jnp.int32), axis=1)
    slot = dest * held_most + rank
    slots_all = n_sky * held_most
    pick = jnp.arange(slots_all)[:, None] == slot[None, :]
    slot_offset = jnp.sum(jnp.where(pick, offsets[None, :] + 1, 0), axis=1) - 1
    pick_half = pick.astype(jnp.bfloat16)
    send_image = jnp.dot(
        pick_half, images.reshape(count, tile * tile), preferred_element_type=jnp.float32
    )
    send_image = send_image.astype(jnp.bfloat16).reshape(n_sky, held_most, tile, tile)
    send_var = jnp.dot(
        pick_half, variance.reshape(count, tile * tile), preferred_element_type=jnp.float32
    )
    send_var = send_var.astype(jnp.bfloat16).reshape(n_sky, held_most, tile, tile)
    send_coef = jnp.dot(pick_half, coeffs, preferred_element_type=jnp.float32)
    send_coef = send_coef.astype(jnp.bfloat16).reshape(n_sky, held_most, BASIS)
    send_place = slot_offset.reshape(n_sky, held_most)
    part_image = lax.all_to_all(send_image, "sky", split_axis=0, concat_axis=0, tiled=True)
    part_var = lax.all_to_all(send_var, "sky", split_axis=0, concat_axis=0, tiled=True)
    part_coef = lax.all_to_all(send_coef, "sky", split_axis=0, concat_axis=0, tiled=True)
    part_place = lax.all_to_all(send_place, "sky", split_axis=0, concat_axis=0, tiled=True)
    sources, held = part_place.shape
    flat_place = part_place.reshape(sources * held)
    results = weigh(
        part_image.reshape(sources * held, tile, tile),
        part_var.reshape(sources * held, tile, tile),
        part_coef.reshape(sources * held, BASIS),
        flat_place >= 0,
        row_side,
        col_side,
    )
    got_image = results[0].reshape(sources, held, tile, tile)
    got_var = results[1].reshape(sources, held, tile, tile)
    got_weight = results[2].reshape(sources, held)
    got_coef = results[3].reshape(sources, held, BASIS)
    received = part_place.shape[0] * part_place.shape[1]
    place_flat = part_place.reshape(received)
    place_pick = (jnp.arange(GRID * GRID)[:, None] == place_flat[None, :]).astype(jnp.float32)
    high = lax.Precision.HIGHEST
    image_pos = jnp.dot(place_pick, got_image.reshape(received, tile * tile), precision=high)
    var_pos = jnp.dot(place_pick, got_var.reshape(received, tile * tile), precision=high)
    weight_pos = jnp.dot(place_pick, got_weight.reshape(received), precision=high)
    psf_part = jnp.sum(got_coef.reshape(received, BASIS), axis=0)
    weight_part = jnp.sum(got_weight)

    def layout(field):
        return (
            field.reshape(GRID, GRID, tile, tile)
            .transpose(0, 2, 1, 3)
            .reshape(patch_side, patch_side)
        )

    weight_cols = jnp.repeat(weight_pos.reshape(GRID, GRID), tile, axis=1)
    image_share, var_share, weight_share = (
        lax.psum_scatter(layout(image_pos), "visit", scatter_dimension=1, tiled=True),
        lax.psum_scatter(layout(var_pos), "visit", scatter_dimension=1, tiled=True),
        lax.psum_scatter(weight_cols, "visit", scatter_dimension=1, tiled=True),
    )
    denom = jnp.maximum(jnp.repeat(weight_share, tile, axis=0), weight_floor)
    coadd_image = image_share / denom
    coadd_variance = var_share / (denom * denom)
    psf_total, weight_total = lax.psum((psf_part, weight_part), "visit")
    share = psf_total / weight_total
    coadd_psf = jnp.einsum(
        "k,ka,kb->ab",
        share,
        col_taps.astype(jnp.float32),
        row_taps.astype(jnp.float32),
        precision=high,
    )[None]
    return (coadd_image, coadd_variance, coadd_psf)


def solution(mesh):
    return jax.shard_map(
        shards,
        mesh=mesh,
        in_specs=(
            P("visit", "sky", None, None),
            P("visit", "sky", None, None),
            P("visit", "sky", None),
            P("visit", "sky", None),
            P("visit", "sky"),
            P(),
            P(),
        ),
        out_specs=(P("sky", "visit"), P("sky", "visit"), P("sky", None, None)),
        check_vma=False,
    )
```

profile of v0, /device:TPU:0, one launch (start us, length us, event | category | flops | bytes accessed | tf_op | source)
XLA Modules:
  0.0 296.3 jit_solution(13076839153214185208)
XLA Ops:
  10.2 7.3 %all-to-all-start = ((s32[8,1,8]{2,1,0:T(1,128)}), s32[8,1,8]{2,1,0:T(1,128)S(1)}, u32[]{:S(2)}, u32[]{:S(2)}) async-start(s32[8,1,8]{2,1,0:T(1,128)} %bitcast.13), calls=%async_computation | async-start | bytes 8192 | tf_op jit(solution)/shard_map/all_to_all | solution.py:86
  17.5 3.5 %fusion.18 = bf16[8,8,128,128]{3,1,2,0:T(8,128)(2,1)} fusion(bf16[4,8,128,128]{3,2,1,0:T(8,128)(2,1)} %bitcast.149, s32[32]{0:T(128)S(1)} %multiply_add_fusion.1), kind=kOutput, calls=%fused_computation.29 | convolution fusion | flops 68159488 | bytes 3145856 | tf_op jit(solution)/shard_map/dot_general | solution.py:76
  21.0 2.9 all-to-all-done
  23.9 3.6 %all-to-all-start.1 = ((bf16[8,8,128,128]{3,1,2,0:T(8,128)(2,1)}), bf16[8,8,128,128]{3,1,2,0:T(8,128)(2,1)S(1)}, u32[]{:S(2)}, u32[]{:S(2)}) async-start(bf16[8,8,128,128]{3,1,2,0:T(8,128)(2,1)} %fusion.18), calls=%async_computation.1 | async-start | bytes 4194304 | tf_op jit(solution)/shard_map/all_to_all | solution.py:84
  27.5 2.2 fusion.19
  29.7 44.9 %all-to-all-done.1 = bf16[8,8,128,128]{3,1,2,0:T(8,128)(2,1)S(1)} async-done(((bf16[8,8,128,128]{3,1,2,0:T(8,128)(2,1)}), bf16[8,8,128,128]{3,1,2,0:T(8,128)(2,1)S(1)}, u32[]{:S(2)}, u32[]{:S(2)}) %all-to-all-start.1) | async-done | bytes 2097184 | tf_op jit(solution)/shard_map/all_to_all | solution.py:84
  74.6 4.4 %all-to-all-start.2 = ((bf16[8,8,128,128]{3,1,2,0:T(8,128)(2,1)}), bf16[8,8,128,128]{3,1,2,0:T(8,128)(2,1)}, u32[]{:S(2)}, u32[]{:S(2)}) async-start(bf16[8,8,128,128]{3,1,2,0:T(8,128)(2,1)} %fusion.19), calls=%async_computation.2 | async-start | bytes 4194304 | tf_op jit(solution)/shard_map/all_to_all | solution.py:83
  83.8 43.1 %all-to-all-done.2 = bf16[8,8,128,128]{3,1,2,0:T(8,128)(2,1)} async-done(((bf16[8,8,128,128]{3,1,2,0:T(8,128)(2,1)}), bf16[8,8,128,128]{3,1,2,0:T(8,128)(2,1)}, u32[]{:S(2)}, u32[]{:S(2)}) %all-to-all-start.2) | async-done | bytes 2097184 | tf_op jit(solution)/shard_map/all_to_all | solution.py:83
  126.8 3.6 %all-to-all-start.3 = ((bf16[8,8,9]{2,1,0:T(8,128)(2,1)}), bf16[8,8,9]{2,1,0:T(8,128)(2,1)S(1)}, u32[]{:S(2)}, u32[]{:S(2)}) async-start(bf16[8,8,9]{2,1,0:T(8,128)(2,1)} %bitcast.23), calls=%async_computation.3 | async-start | bytes 32768 | tf_op jit(solution)/shard_map/all_to_all | solution.py:85
  131.4 3.5 %copy.52 = bf16[8,8,128,128]{3,2,1,0:T(8,128)(2,1)} copy(bf16[8,8,128,128]{3,1,2,0:T(8,128)(2,1)} %all-to-all-done.2) | data formatting | bytes 4194304 | tf_op jit(solution)/shard_map/all_to_all | solution.py:83
  134.9 2.2 all-to-all-done.3
  137.0 35.6 %while.10 = (s32[]{:T(128)}, f32[4,16,128,128]{3,2,1,0:T(8,128)}, bf16[4,16,128,128]{3,2,1,0:T(8,128)(2,1)}, bf16[128,1152]{0,1:T(8,128)(2,1)S(1)}, bf16[4,16,9]...) while((s32[]{:T(128)}, f32[4,16,128,128]{3,2,1,0:T(8,128)}, ...), condition=%wide.region_4.5_spmd, body=%wide.region_3.4_spmd.sunk | while | flops 1212678272 | bytes 25233904 | solution.py:33
  137.0 2.4 multiply_convert_fusion.2
  139.5 3.0 %copy.109 = bf16[16,128,9,128]{3,0,2,1:T(8,128)(2,1)S(1)} copy(bf16[16,128,9,128]{3,1,2,0:T(8,128)(2,1)S(1)} %multiply_convert_fusion.2) | data formatting | bytes 9437184 | tf_op jit(solution)/shard_map/while/body/eval_jaxpr/vmap()/convert_element_type | solution.py:28
  142.5 2.0 fusion.63
  145.9 2.4 multiply_convert_fusion.2
  148.4 3.0 %copy.109 = bf16[16,128,9,128]{3,0,2,1:T(8,128)(2,1)S(1)} copy(bf16[16,128,9,128]{3,1,2,0:T(8,128)(2,1)S(1)} %multiply_convert_fusion.2) | data formatting | bytes 9437184 | tf_op jit(solution)/shard_map/while/body/eval_jaxpr/vmap()/convert_element_type | solution.py:28
  151.4 2.0 fusion.63
  154.9 2.4 multiply_convert_fusion.2
  157.3 3.0 %copy.109 = bf16[16,128,9,128]{3,0,2,1:T(8,128)(2,1)S(1)} copy(bf16[16,128,9,128]{3,1,2,0:T(8,128)(2,1)S(1)} %multiply_convert_fusion.2) | data formatting | bytes 9437184 | tf_op jit(solution)/shard_map/while/body/eval_jaxpr/vmap()/convert_element_type | solution.py:28
  160.4 2.0 fusion.63
  163.8 2.4 multiply_convert_fusion.2
  166.2 3.0 %copy.109 = bf16[16,128,9,128]{3,0,2,1:T(8,128)(2,1)S(1)} copy(bf16[16,128,9,128]{3,1,2,0:T(8,128)(2,1)S(1)} %multiply_convert_fusion.2) | data formatting | bytes 9437184 | tf_op jit(solution)/shard_map/while/body/eval_jaxpr/vmap()/convert_element_type | solution.py:28
  174.1 7.8 %fusion.10 = (f32[8,128,8,128]{3,2,1,0:T(8,128)}, f32[8,128,8,128]{3,2,1,0:T(8,128)S(1)}) fusion(bf16[8,8,128,128]{3,1,2,0:T(8,128)(2,1)} %copy-done.1, f32[64]{0:T(128)S(1)} %get-tuple-element.97, f32[8,8,128,128]{3,2,1,0:T(8,128)} %bitcast.148, f32[64]{0:T(128)S(1)} %get-tuple-element.98), kind=kLoop, calls=%fused_computation.15 | loop fusion | flops 3145728 | bytes 14680576
  181.9 2.5 fusion.14
  184.5 2.9 copy.104
  187.5 4.5 %fusion.12 = f32[8,8,128,128]{3,1,2,0:T(8,128)S(1)} fusion(f32[8,128,8,128]{3,2,1,0:T(8,128)} %get-tuple-element.102, s32[64]{0:T(128)S(1)} %eq.92, s32[8,8]{1,0:T(8,128)S(1)} %multiply_add_fusion), kind=kOutput, calls=%fused_computation.21 | convolution fusion | flops 805310464 | bytes 8389120 | tf_op jit(solution)/shard_map/dot_general | solution.py:106
  192.0 3.0 %copy.103 = f32[128,8,8,128]{3,1,2,0:T(8,128)} copy(f32[128,8,8,128]{3,2,1,0:T(8,128)S(1)} %bitcast.144) | data formatting | bytes 8388608
  195.1 6.3 %all-reduce = (f32[9]{0:T(128)S(1)}, f32[]{:T(128)}) all-reduce(f32[9]{0:T(128)S(1)} %multiply_reduce_fusion, f32[]{:T(128)} %get-tuple-element.95), channel_id=1, replica_groups=mesh['sky'=8,'visit'=4] {'visit'}, use_global_device_ids=true, to_apply=%region_9.10 | all-reduce | flops 10 | bytes 80 | tf_op jit(solution)/shard_map/psum | solution.py:127
  203.7 36.0 %reduce-scatter.4.cloned.1.call-done = f32[1024,256]{1,0:T(8,128)} async-done(((f32[1024,1024]{1,0:T(8,128)}), f32[1024,256]{1,0:T(8,128)}) %reduce-scatter.4.cloned.1.call-update) | async-done | bytes 1048592 | tf_op jit(solution)/shard_map/reduce_scatter | solution.py:120
  239.6 47.1 %reduce-scatter.8.cloned.1.call-done = f32[1024,256]{1,0:T(8,128)} async-done(((f32[1024,1024]{1,0:T(8,128)}), f32[1024,256]{1,0:T(8,128)}) %reduce-scatter.8.cloned.1.call-update) | async-done | bytes 1048592 | tf_op jit(solution)/shard_map/reduce_scatter | solution.py:121
  286.7 3.0 %fusion.26 = (f32[1024,256]{1,0:T(8,128)}, f32[1024,256]{1,0:T(8,128)}) fusion(f32[1024,256]{1,0:T(8,128)} %reduce-scatter.8.cloned.1.call-done, f32[8,256]{1,0:T(8,128)S(1)} %broadcast_maximum_fusion, f32[1024,256]{1,0:T(8,128)} %reduce-scatter.4.cloned.1.call-done), kind=kLoop, calls=%fused_computation.41 | loop fusion | flops 786432 | bytes 4202496 | tf_op jit(solution)/shard_map/div | solution.py:126
  (61 shorter events, 20.2 us)
Async XLA Ops:
  7.2 73.8 %copy-start = (bf16[9,41]{1,0:T(8,128)(2,1)S(1)}, bf16[9,41]{1,0:T(8,128)(2,1)}, u32[]{:S(2)}) copy-start(bf16[9,41]{1,0:T(8,128)(2,1)} %param.14) | copy-start | bytes 2218
  7.2 20.3 %copy-start.2 = (bf16[1,32,128,128]{3,2,1,0:T(8,128)(2,1)S(1)}, bf16[1,32,128,128]{3,2,1,0:T(8,128)(2,1)}, u32[]{:S(2)}) copy-start(bf16[1,32,128,128]{3,2,1,0:T(8,128)(2,1)} %param.9) | copy-start | bytes 3145732
  10.2 13.6 %all-to-all-start = ((s32[8,1,8]{2,1,0:T(1,128)}), s32[8,1,8]{2,1,0:T(1,128)S(1)}, u32[]{:S(2)}, u32[]{:S(2)}) async-start(s32[8,1,8]{2,1,0:T(1,128)} %bitcast.13), calls=%async_computation | async-start | bytes 8192 | tf_op jit(solution)/shard_map/all_to_all | solution.py:86
  23.9 50.8 %all-to-all-start.1 = ((bf16[8,8,128,128]{3,1,2,0:T(8,128)(2,1)}), bf16[8,8,128,128]{3,1,2,0:T(8,128)(2,1)S(1)}, u32[]{:S(2)}, u32[]{:S(2)}) async-start(bf16[8,8,128,128]{3,1,2,0:T(8,128)(2,1)} %fusion.18), calls=%async_computation.1 | async-start | bytes 4194304 | tf_op jit(solution)/shard_map/all_to_all | solution.py:84
  27.5 51.5 %copy-start.3 = (bf16[1,32,9]{1,2,0:T(8,128)(2,1)S(1)}, bf16[1,32,9]{1,2,0:T(8,128)(2,1)}, u32[]{:S(2)}) copy-start(bf16[1,32,9]{1,2,0:T(8,128)(2,1)} %param.11) | copy-start | bytes 1732
  27.5 52.4 %copy-start.4 = (bf16[9,41]{1,0:T(8,128)(2,1)S(1)}, bf16[9,41]{1,0:T(8,128)(2,1)}, u32[]{:S(2)}) copy-start(bf16[9,41]{1,0:T(8,128)(2,1)} %param.15) | copy-start | bytes 2218
  74.6 9.1 %copy-start.1 = (bf16[8,8,128,128]{3,1,2,0:T(8,128)(2,1)}, bf16[8,8,128,128]{3,1,2,0:T(8,128)(2,1)S(1)}, u32[]{:S(2)}) copy-start(bf16[8,8,128,128]{3,1,2,0:T(8,128)(2,1)S(1)} %all-to-all-done.1) | copy-start | bytes 6291460
  74.6 52.2 %all-to-all-start.2 = ((bf16[8,8,128,128]{3,1,2,0:T(8,128)(2,1)}), bf16[8,8,128,128]{3,1,2,0:T(8,128)(2,1)}, u32[]{:S(2)}, u32[]{:S(2)}) async-start(bf16[8,8,128,128]{3,1,2,0:T(8,128)(2,1)} %fusion.19), calls=%async_computation.2 | async-start | bytes 4194304 | tf_op jit(solution)/shard_map/all_to_all | solution.py:83
  126.8 10.2 %all-to-all-start.3 = ((bf16[8,8,9]{2,1,0:T(8,128)(2,1)}), bf16[8,8,9]{2,1,0:T(8,128)(2,1)S(1)}, u32[]{:S(2)}, u32[]{:S(2)}) async-start(bf16[8,8,9]{2,1,0:T(8,128)(2,1)} %bitcast.23), calls=%async_computation.3 | async-start | bytes 32768 | tf_op jit(solution)/shard_map/all_to_all | solution.py:85
  130.4 72.5 %reduce-scatter.6.cloned.1.call-start = ((), (), s32[]{:S(2)}) async-start(), calls=%async_computation.8 | async-start | bytes 40960 | tf_op jit(solution)/shard_map/reduce_scatter | solution.py:122
  173.9 65.8 %reduce-scatter.4.cloned.1.call-start = ((), (), s32[]{:S(2)}) async-start(), calls=%async_computation.7 | async-start | bytes 5242880 | tf_op jit(solution)/shard_map/reduce_scatter | solution.py:120
  187.4 99.3 %reduce-scatter.8.cloned.1.call-start = ((), (), s32[]{:S(2)}) async-start(), calls=%async_computation.9 | async-start | bytes 5242880 | tf_op jit(solution)/shard_map/reduce_scatter | solution.py:121
Sparse Core Ops, SparseCore 0:
  174.0 18.3 reduce-scatter.5
  195.1 44.5 reduce-scatter.3
  242.2 44.5 reduce-scatter.7
where the time goes:
time: 297 us; the launch traced here: 296 us
  waiting for transfers between devices  176 us (59%)
  matrix products  32.7 us (11%)
  local copies, waits for them, and re-layouts  31.4 us (11%)
  starting transfers between devices  19.4 us (7%)
  other arithmetic  16.4 us (6%)
  between operations  13.9 us (5%)
  blocking collectives  6.3 us (2%)
    reduce_scatter x1, waiting for transfers between devices, shards(): lax.psum_scatter(layout(var_pos), 'visit', scatter_dimension=1, tiled=True)  47.1 us
    all_to_all x1, waiting for transfers between devices, shards(): lax.all_to_all(send_var, 'sky', split_axis=0, concat_axis=0, tiled=True)  44.9 us
    all_to_all x1, waiting for transfers between devices, shards(): lax.all_to_all(send_image, 'sky', split_axis=0, concat_axis=0, tiled=True)  43.1 us
    reduce_scatter x1, waiting for transfers between devices, shards(): lax.psum_scatter(layout(image_pos), 'visit', scatter_dimension=1, tiled=T...  36 us
    convert_element_type x4, local copies, waits for them, and re-layouts, single(): (first * coeff.astype(jnp.float32)[None, :, None]).astype(jnp.bfloat16)  12.2 us
    dot_general x4, matrix products, single(): jnp.dot(image, row_side, preferred_element_type=jnp.float32)  9.75 us
    dot_general x4, matrix products, single(): jnp.dot(col_side, scaled.reshape(tile * BASIS, tile), preferred_element_t...  7.96 us
    unnamed x1, other arithmetic  7.82 us
  transfers between devices with their start and end apart: 7, of which 6 were waited for; matrix products, arithmetic and copies ran while one was open for 13% of the time, Pallas kernels for 0%

commit v1 on v0

v1 whole, which is shorter than its diff:
```python
import jax
import jax.numpy as jnp
from jax import lax
from jax.experimental import pallas as pl
from jax.experimental.pallas import tpu as pltpu
from jax.sharding import PartitionSpec as P

GRID = 8
BASIS = 9
META = 16
EXTRA = 8


weight_floor = 0.5


def band_table(taps, tile):
    span = taps.shape[1]
    offset = jnp.arange(tile)[:, None] - jnp.arange(tile)[None, :] + (span - 1) // 2
    select = (offset[None, :, :] == jnp.arange(span)[:, None, None]).astype(jnp.float32)
    return jnp.einsum("kt,tij->kij", taps.astype(jnp.float32), select).astype(jnp.bfloat16)


def variance_kernel(place_ref, w2_ref, var_ref, extra_ref, out_ref):
    slots = var_ref.shape[0]
    tile = var_ref.shape[2]
    positions = out_ref.shape[0]
    out_ref[:, :tile, :] = jnp.zeros((positions, tile, tile), jnp.float32)
    out_ref[:, tile:, :] = extra_ref[...]

    def body(t, carry):
        q = place_ref[t]

        @pl.when(q >= 0)
        def _():
            out_ref[q, :tile, :] += w2_ref[t] * var_ref[t, :tile, :].astype(jnp.float32)

        return carry

    lax.fori_loop(0, slots, body, 0)


def image_kernel(place_ref, w_ref, coef_ref, img_ref, row_ref, col_ref, out_ref):
    slots = img_ref.shape[0]
    tile = img_ref.shape[2]
    out_ref[...] = jnp.zeros(out_ref.shape, jnp.float32)

    def body(t, carry):
        q = place_ref[t]

        @pl.when(q >= 0)
        def _():
            first = jnp.dot(img_ref[t], row_ref[...], preferred_element_type=jnp.float32)
            scaled = jnp.concatenate(
                [
                    (first[:, k * tile:(k + 1) * tile] * coef_ref[t * BASIS + k]).astype(jnp.bfloat16)
                    for k in range(BASIS)
                ],
                axis=0,
            )
            matched = jnp.dot(col_ref[...], scaled, preferred_element_type=jnp.float32)
            out_ref[q] += w_ref[t] * matched

        return carry

    lax.fori_loop(0, slots, body, 0)


def smem():
    return pl.BlockSpec(memory_space=pltpu.SMEM)


def vmem():
    return pl.BlockSpec(memory_space=pltpu.VMEM)


def variance_field(place, w2, var_meta, extra):
    positions, extra_rows, tile = extra.shape
    return pl.pallas_call(
        variance_kernel,
        out_shape=jax.ShapeDtypeStruct((positions, tile + extra_rows, tile), jnp.float32),
        in_specs=[smem(), smem(), vmem(), vmem()],
        out_specs=vmem(),
    )(place, w2, var_meta, extra)


def image_field(place, w, coef, images, row_side, col_side, positions):
    tile = images.shape[2]
    return pl.pallas_call(
        image_kernel,
        out_shape=jax.ShapeDtypeStruct((positions, tile, tile), jnp.float32),
        in_specs=[smem(), smem(), smem(), vmem(), vmem(), vmem()],
        out_specs=vmem(),
    )(place, w, coef, images, row_side, col_side)


def shards(tile_image, tile_variance, match_coeffs, tile_patch, tile_offset, row_taps, col_taps):
    n_sky = lax.axis_size("sky")
    n_visit = lax.axis_size("visit")
    images = tile_image[0]
    variance = tile_variance[0]
    coeffs = match_coeffs[0]
    count = images.shape[0]
    tile = images.shape[1]
    held_most = max(2, 2 * count // n_sky)
    positions = GRID * GRID
    dest = tile_patch[0, :, 0]
    offsets = tile_offset[0]
    band_row = band_table(row_taps, tile)
    band_col = band_table(col_taps, tile)
    row_side = band_row.transpose(1, 0, 2).reshape(tile, BASIS * tile)
    col_side = band_col.transpose(2, 0, 1).reshape(tile, BASIS * tile)
    order = jnp.arange(count)
    earlier = (dest[:, None] == dest[None, :]) & (order[None, :] < order[:, None])
    rank = jnp.sum(earlier.astype(jnp.int32), axis=1)
    slot = dest * held_most + rank
    slots_all = n_sky * held_most
    pick = (jnp.arange(slots_all)[:, None] == slot[None, :]).astype(jnp.bfloat16)
    column_major = (offsets % GRID) * GRID + offsets // GRID
    meta_row = jnp.concatenate(
        [
            coeffs.astype(jnp.float32),
            (column_major + 1).astype(jnp.float32)[:, None],
            jnp.zeros((count, tile - BASIS - 1), jnp.float32),
        ],
        axis=1,
    )
    meta = jnp.concatenate(
        [meta_row[:, None, :], jnp.zeros((count, META - 1, tile), jnp.float32)], axis=1
    ).astype(jnp.bfloat16)
    var_meta = jnp.concatenate([variance, meta], axis=1)
    send_vm = jnp.dot(
        pick, var_meta.reshape(count, (tile + META) * tile), preferred_element_type=jnp.float32
    )
    send_vm = send_vm.astype(jnp.bfloat16).reshape(n_sky, held_most, tile + META, tile)
    send_image = jnp.dot(
        pick, images.reshape(count, tile * tile), preferred_element_type=jnp.float32
    )
    send_image = send_image.astype(jnp.bfloat16).reshape(n_sky, held_most, tile, tile)

    part_vm = lax.all_to_all(send_vm, "sky", split_axis=0, concat_axis=0, tiled=True)
    part_vm = part_vm.reshape(slots_all, tile + META, tile)
    got_meta = part_vm[:, tile, :].astype(jnp.float32)
    got_coef = got_meta[:, :BASIS]
    place = got_meta[:, BASIS].astype(jnp.int32) - 1
    valid = place >= 0
    mean_var = jnp.mean(part_vm[:, :tile, :].astype(jnp.float32), axis=(1, 2))
    weight = jnp.where(valid, 1.0 / jnp.where(valid, mean_var, 1.0), 0.0)
    psf_part = jnp.sum(weight[:, None] * got_coef, axis=0)
    weight_part = jnp.sum(weight)
    weight_pos = jnp.sum(
        jnp.where(jnp.arange(positions)[:, None] == place[None, :], weight[None, :], 0.0), axis=1
    )
    psf_row = jnp.concatenate(
        [psf_part, weight_part[None], jnp.zeros((tile - BASIS - 1,), jnp.float32)]
    )
    extra = jnp.concatenate(
        [
            jnp.broadcast_to(weight_pos[:, None, None], (positions, 1, tile)),
            jnp.broadcast_to(psf_row[None, None, :], (positions, 1, tile)),
            jnp.zeros((positions, EXTRA - 2, tile), jnp.float32),
        ],
        axis=1,
    )
    var_pos = variance_field(place, weight * weight, part_vm, extra)
    var_share = lax.psum_scatter(
        var_pos.reshape(GRID, GRID, tile + EXTRA, tile), "visit", scatter_dimension=0, tiled=True
    )

    part_image = lax.all_to_all(send_image, "sky", split_axis=0, concat_axis=0, tiled=True)
    part_image = part_image.reshape(slots_all, tile, tile)
    coef_flat = got_coef.reshape(slots_all * BASIS)
    image_pos = image_field(place, weight, coef_flat, part_image, row_side, col_side, positions)
    image_share = lax.psum_scatter(
        image_pos.reshape(GRID, GRID, tile, tile), "visit", scatter_dimension=0, tiled=True
    )

    per_dev = GRID // n_visit
    denom = jnp.maximum(var_share[:, :, tile, 0], weight_floor)[:, :, None, None]
    coadd_image = image_share / denom
    coadd_variance = var_share[:, :, :tile, :] / (denom * denom)

    def layout(field):
        return field.transpose(1, 2, 0, 3).reshape(GRID * tile, per_dev * tile)

    psf_total = var_share[0, 0, tile + 1, :BASIS]
    weight_total = var_share[0, 0, tile + 1, BASIS]
    share = psf_total / weight_total
    high = lax.Precision.HIGHEST
    coadd_psf = jnp.einsum(
        "k,ka,kb->ab",
        share,
        col_taps.astype(jnp.float32),
        row_taps.astype(jnp.float32),
        precision=high,
    )[None]
    return (layout(coadd_image), layout(coadd_variance), coadd_psf)


def solution(mesh):
    return jax.shard_map(
        shards,
        mesh=mesh,
        in_specs=(
            P("visit", "sky", None, None),
            P("visit", "sky", None, None),
            P("visit", "sky", None),
            P("visit", "sky", None),
            P("visit", "sky"),
            P(),
            P(),
        ),
        out_specs=(P("sky", "visit"), P("sky", "visit"), P("sky", None, None)),
        check_vma=False,
    )
```

time: 297 us -> 232 us (0.78)
  matrix products: 32.7 us -> 3.25 us
  waiting for transfers between devices: 176 us -> 158 us
  Pallas kernels: 0 us -> 16.4 us
  local copies, waits for them, and re-layouts: 31.4 us -> 16.2 us
  starting transfers between devices: 19.4 us -> 11.1 us
  blocking collectives: 6.3 us -> 0 us
  other arithmetic: 16.4 us -> 11.6 us
    dot_general x14 -> x2, matrix products: 31 us -> 1.57 us  [the longest x1 0.81 us: shards(): jnp.dot(pick, images.reshape(count, tile * tile), preferred_element_type=...]
    reduce_scatter x3 -> x2, waiting for transfers between devices: 83.1 us -> 60.3 us  [the longest x1 60.3 us: shards(): lax.psum_scatter(image_pos.reshape(GRID, GRID, tile, tile), 'visit', scat...]
    pallas_call x0 -> x2, Pallas kernels: none -> 16.4 us  [the longest x1 11.3 us: image_field(): pl.pallas_call(image_kernel, out_shape=jax.ShapeDtypeStruct((positions, t...]
    convert_element_type x4 -> x0, local copies, waits for them, and re-layouts: 12.2 us -> none  [single(): (first * coeff.astype(jnp.float32)[None, :, None]).astype(jnp.bfloat16)]
    unnamed x1 -> x0, other arithmetic: 7.82 us -> none
    all_to_all x3 -> x1, starting transfers between devices: 14.5 us -> 7.25 us  [shards(): lax.all_to_all(send_vm, 'sky', split_axis=0, concat_axis=0, tiled=True)]
    psum x1 -> x0, blocking collectives: 6.3 us -> none  [shards(): psf_total, weight_total = lax.psum((psf_part, weight_part), 'visit')]
    dynamic_update_slice x8 -> x0, local copies, waits for them, and re-layouts: 5.63 us -> none  [match_tiles(): return lax.map(single, (images, coeffs), batch_size=16)]
  transfers between devices with their start and end apart: 7 -> 4, of which waited for: 6 -> 3; matrix products, arithmetic and copies ran while one was open for 13% -> 4% of each run, Pallas kernels for 0% -> 5%
where the time goes in v1:
time: 232 us; the launch traced here: 231 us
  waiting for transfers between devices  158 us (68%)
  Pallas kernels  16.4 us (7%)
  local copies, waits for them, and re-layouts  16.2 us (7%)
  between operations  14.2 us (6%)
  other arithmetic  11.6 us (5%)
  starting transfers between devices  11.1 us (5%)
  matrix products  3.25 us (1%)
    reduce_scatter x1, waiting for transfers between devices, shards(): lax.psum_scatter(image_pos.reshape(GRID, GRID, tile, tile), 'visit', scat...  60.3 us
    all_to_all x1, waiting for transfers between devices, shards(): lax.all_to_all(send_vm, 'sky', split_axis=0, concat_axis=0, tiled=True)  53.7 us
    all_to_all x1, waiting for transfers between devices, shards(): lax.all_to_all(send_image, 'sky', split_axis=0, concat_axis=0, tiled=True)  44 us
    pallas_call x1, Pallas kernels, image_field(): pl.pallas_call(image_kernel, out_shape=jax.ShapeDtypeStruct((positions, t...  11.3 us
    all_to_all x1, starting transfers between devices, shards(): lax.all_to_all(send_vm, 'sky', split_axis=0, concat_axis=0, tiled=True)  7.25 us
    unnamed x19, local copies, waits for them, and re-layouts  6.1 us
    pallas_call x1, Pallas kernels, variance_field(): pl.pallas_call(variance_kernel, out_shape=jax.ShapeDtypeStruct((positions...  5.02 us
  transfers between devices with their start and end apart: 4, of which 3 were waited for; matrix products, arithmetic and copies ran while one was open for 4% of the time, Pallas kernels for 5%

profile of v1, /device:TPU:0, one launch (start us, length us, event | category | flops | bytes accessed | tf_op | source)
XLA Modules:
  0.0 230.7 jit_solution(9758212334419076038)
XLA Ops:
  7.2 0.9 convert_reduce_fusion.1
  8.8 0.7 convert_convert_fusion
  9.5 0.8 copy.32
  10.5 1.3 fusion.11
  11.8 0.8 fusion.3
  12.6 1.8 copy.35
  14.4 7.3 %all-to-all-start = ((bf16[8,8,144,128]{3,2,1,0:T(8,128)(2,1)}), bf16[8,8,144,128]{3,2,1,0:T(8,128)(2,1)S(1)}, u32[]{:S(2)}, u32[]{:S(2)}) async-start(bf16[8,8,144,128]{3,2,1,0:T(8,128)(2,1)} %copy.35), calls=%async_computation | async-start | bytes 4718592 | tf_op jit(solution)/shard_map/all_to_all | solution.py:141
  21.8 53.7 %all-to-all-done = bf16[8,8,144,128]{3,2,1,0:T(8,128)(2,1)S(1)} async-done(((bf16[8,8,144,128]{3,2,1,0:T(8,128)(2,1)}), bf16[8,8,144,128]{3,2,1,0:T(8,128)(2,1)S(1)}, u32[]{:S(2)}, u32[]{:S(2)}) %all-to-all-start) | async-done | bytes 2359328 | tf_op jit(solution)/shard_map/all_to_all | solution.py:141
  77.9 0.7 pad_maximum_fusion
  78.8 0.8 maximum_maximum_fusion.extra_ref
  79.6 5.0 %shard_map.95 = f32[64,136,128]{2,1,0:T(8,128)} custom-call(s32[64]{0:T(128)} %copy-done.4, f32[64]{0:T(128)} %mul.37.w2_ref, bf16[64,144,128]{2,1,0:T(8,128)(2,1)} %bitcast.76, f32[64,8,128]{2,1,0:T(8,128)} %maximum_maximum_fusion.extra_ref), custom_call_target="tpu_custom_call" | custom-call | tf_op jit(solution)/shard_map/pallas_call | solution.py:79
  84.7 1.2 copy-done.3
  85.9 0.8 fusion.4
  86.7 1.9 copy.36
  88.6 3.8 %all-to-all-start.1 = ((bf16[8,8,128,128]{3,2,1,0:T(8,128)(2,1)}), bf16[8,8,128,128]{3,2,1,0:T(8,128)(2,1)S(1)}, u32[]{:S(2)}, u32[]{:S(2)}) async-start(bf16[8,8,128,128]{3,2,1,0:T(8,128)(2,1)} %copy.36), calls=%async_computation.1 | async-start | bytes 4194304 | tf_op jit(solution)/shard_map/all_to_all | solution.py:170
  92.5 0.7 fusion.10
  93.5 0.9 copy.39.row_ref
  94.4 0.7 fusion.9
  95.2 0.9 copy.40.col_ref
  96.1 0.7 reshape.216.coef_ref
  96.8 44.0 %all-to-all-done.1 = bf16[8,8,128,128]{3,2,1,0:T(8,128)(2,1)S(1)} async-done(((bf16[8,8,128,128]{3,2,1,0:T(8,128)(2,1)}), bf16[8,8,128,128]{3,2,1,0:T(8,128)(2,1)S(1)}, u32[]{:S(2)}, u32[]{:S(2)}) %all-to-all-start.1) | async-done | bytes 2097184 | tf_op jit(solution)/shard_map/all_to_all | solution.py:170
  140.8 1.4 copy-done.2
  142.2 11.3 %shard_map.94 = f32[64,128,128]{2,1,0:T(8,128)} custom-call(s32[64]{0:T(128)} %copy-done.4, f32[64]{0:T(128)} %copy-done.5, f32[576]{0:T(1024)} %reshape.216.coef_ref, bf16[64,128,128]{2,1,0:T(8,128)(2,1)} %bitcast.79, bf16[128,1152]{1,0:T(8,128)(2,1)} %copy.39.row_ref, bf16[128,1152]{1,0:T(8,128)(2,1)} %copy.40.col_ref), custom_call_target="tpu_custom_call" | custom-call | tf_op jit(solution)/shard_map/pallas_call | solution.py:89
  153.6 1.0 multiply_reduce_fusion.1
  154.6 60.3 %reduce-scatter.3.cloned.1.call-done = f32[2,8,128,128]{3,2,1,0:T(8,128)} async-done(((f32[8,8,128,128]{3,2,1,0:T(8,128)}), f32[2,8,128,128]{3,2,1,0:T(8,128)}) %reduce-scatter.3.cloned.1.call-update) | async-done | bytes 1048592 | tf_op jit(solution)/shard_map/reduce_scatter | solution.py:174
  214.8 1.8 fusion.16
  216.6 0.8 copy.43
  217.5 1.0 copy.60
  218.5 0.8 copy.42
  219.3 1.0 copy.61
  220.4 1.3 slice.39
  221.6 1.3 fusion.29
  (42 shorter events, 5.1 us)
Async XLA Ops:
  7.2 85.3 %copy-start = (bf16[9,41]{1,0:T(8,128)(2,1)S(1)}, bf16[9,41]{1,0:T(8,128)(2,1)}, u32[]{:S(2)}) copy-start(bf16[9,41]{1,0:T(8,128)(2,1)} %param.12) | copy-start | bytes 2218
  14.4 61.1 %all-to-all-start = ((bf16[8,8,144,128]{3,2,1,0:T(8,128)(2,1)}), bf16[8,8,144,128]{3,2,1,0:T(8,128)(2,1)S(1)}, u32[]{:S(2)}, u32[]{:S(2)}) async-start(bf16[8,8,144,128]{3,2,1,0:T(8,128)(2,1)} %copy.35), calls=%async_computation | async-start | bytes 4718592 | tf_op jit(solution)/shard_map/all_to_all | solution.py:141
  21.6 131.9 %reduce-scatter.5.cloned.1.call-start = ((), (), s32[]{:S(2)}) async-start(), calls=%async_computation.5 | async-start | bytes 5570560 | tf_op jit(solution)/shard_map/reduce_scatter | solution.py:166
  75.5 4.1 %copy-start.1 = (bf16[8,8,144,128]{3,2,1,0:T(8,128)(2,1)}, bf16[8,8,144,128]{3,2,1,0:T(8,128)(2,1)S(1)}, u32[]{:S(2)}) copy-start(bf16[8,8,144,128]{3,2,1,0:T(8,128)(2,1)S(1)} %all-to-all-done) | copy-start | bytes 7077892
  76.3 3.3 %copy-start.4 = (s32[64]{0:T(128)}, s32[64]{0:T(128)S(1)}, u32[]{:S(2)}) copy-start(s32[64]{0:T(128)S(1)} %fusion.18.place_ref) | copy-start | bytes 772
  76.9 7.7 %copy-start.5 = (f32[64]{0:T(128)}, f32[64]{0:T(128)S(1)}, u32[]{:S(2)}) copy-start(f32[64]{0:T(128)S(1)} %get-tuple-element.15.w_ref) | copy-start | bytes 772
  84.6 1.2 copy-start.3
  88.6 5.8 %copy-start.6 = (bf16[9,41]{1,0:T(8,128)(2,1)S(1)}, bf16[9,41]{1,0:T(8,128)(2,1)}, u32[]{:S(2)}) copy-start(bf16[9,41]{1,0:T(8,128)(2,1)} %param.13) | copy-start | bytes 2218
  88.6 52.2 %all-to-all-start.1 = ((bf16[8,8,128,128]{3,2,1,0:T(8,128)(2,1)}), bf16[8,8,128,128]{3,2,1,0:T(8,128)(2,1)S(1)}, u32[]{:S(2)}, u32[]{:S(2)}) async-start(bf16[8,8,128,128]{3,2,1,0:T(8,128)(2,1)} %copy.36), calls=%async_computation.1 | async-start | bytes 4194304 | tf_op jit(solution)/shard_map/all_to_all | solution.py:170
  92.4 122.5 %reduce-scatter.3.cloned.1.call-start = ((), (), s32[]{:S(2)}) async-start(), calls=%async_computation.4 | async-start | bytes 5242880 | tf_op jit(solution)/shard_map/reduce_scatter | solution.py:174
  140.8 1.4 copy-start.2
Sparse Core Ops, SparseCore 0:
  84.8 45.2 reduce-scatter.4
  153.7 61.1 reduce-scatter.2

commit v2 on v1

v2 whole, which is shorter than its diff:
```python
import jax
import jax.numpy as jnp
from jax import lax
from jax.experimental import pallas as pl
from jax.experimental.pallas import tpu as pltpu
from jax.sharding import PartitionSpec as P

GRID = 8
BASIS = 9
META = 16
EXTRA = 8


weight_floor = 0.5


def band_table(taps, tile):
    span = taps.shape[1]
    offset = jnp.arange(tile)[:, None] - jnp.arange(tile)[None, :] + (span - 1) // 2
    select = (offset[None, :, :] == jnp.arange(span)[:, None, None]).astype(jnp.float32)
    return jnp.einsum("kt,tij->kij", taps.astype(jnp.float32), select).astype(jnp.bfloat16)


def place_tile(out_ref, row, group, sub, contrib):
    tile = contrib.shape[0]
    per_dev = out_ref.shape[2] // tile
    start = pl.multiple_of(row * tile, tile)
    for c in range(per_dev):

        @pl.when(sub == c)
        def _():
            out_ref[group, pl.ds(start, tile), c * tile:(c + 1) * tile] += contrib


def variance_kernel(row_ref, group_ref, sub_ref, w2_ref, var_ref, out_ref):
    slots = var_ref.shape[0]
    out_ref[...] = jnp.zeros(out_ref.shape, jnp.float32)

    def body(t, carry):
        row = row_ref[t]

        @pl.when(row >= 0)
        def _():
            contrib = w2_ref[t] * var_ref[t].astype(jnp.float32)
            place_tile(out_ref, row, group_ref[t], sub_ref[t], contrib)

        return carry

    lax.fori_loop(0, slots, body, 0)


def image_kernel(row_ref, group_ref, sub_ref, w_ref, coef_ref, img_ref, row_side_ref, col_side_ref,
                 extra_ref, out_ref):
    slots = img_ref.shape[0]
    tile = img_ref.shape[2]
    body_rows = out_ref.shape[1] - extra_ref.shape[1]
    out_ref[:, :body_rows, :] = jnp.zeros((out_ref.shape[0], body_rows, out_ref.shape[2]), jnp.float32)
    out_ref[:, body_rows:, :] = extra_ref[...]

    def body(t, carry):
        row = row_ref[t]

        @pl.when(row >= 0)
        def _():
            first = jnp.dot(img_ref[t, :tile, :], row_side_ref[...], preferred_element_type=jnp.float32)
            scaled = jnp.concatenate(
                [
                    (first[:, k * tile:(k + 1) * tile] * coef_ref[t * BASIS + k]).astype(jnp.bfloat16)
                    for k in range(BASIS)
                ],
                axis=0,
            )
            matched = jnp.dot(col_side_ref[...], scaled, preferred_element_type=jnp.float32)
            place_tile(out_ref, row, group_ref[t], sub_ref[t], w_ref[t] * matched)

        return carry

    lax.fori_loop(0, slots, body, 0)


def smem():
    return pl.BlockSpec(memory_space=pltpu.SMEM)


def vmem():
    return pl.BlockSpec(memory_space=pltpu.VMEM)


def variance_field(where, w2, var, field_shape):
    return pl.pallas_call(
        variance_kernel,
        out_shape=jax.ShapeDtypeStruct(field_shape, jnp.float32),
        in_specs=[smem(), smem(), smem(), smem(), vmem()],
        out_specs=vmem(),
    )(*where, w2, var)


def image_field(where, w, coef, images, row_side, col_side, extra, field_shape):
    return pl.pallas_call(
        image_kernel,
        out_shape=jax.ShapeDtypeStruct(field_shape, jnp.float32),
        in_specs=[smem(), smem(), smem(), smem(), smem(), vmem(), vmem(), vmem(), vmem()],
        out_specs=vmem(),
        cost_estimate=pl.CostEstimate(
            flops=4 * images.shape[0] * images.shape[2] ** 3 * BASIS,
            transcendentals=0,
            bytes_accessed=images.size * 2 + 4 * (field_shape[0] * field_shape[1] * field_shape[2]),
        ),
    )(*where, w, coef, images, row_side, col_side, extra)


def split_exact(value):
    high = value.astype(jnp.bfloat16)
    rest = value - high.astype(jnp.float32)
    middle = rest.astype(jnp.bfloat16)
    low = (rest - middle.astype(jnp.float32)).astype(jnp.bfloat16)
    return high, middle, low


def shards(tile_image, tile_variance, match_coeffs, tile_patch, tile_offset, row_taps, col_taps):
    n_sky = lax.axis_size("sky")
    n_visit = lax.axis_size("visit")
    images = tile_image[0]
    variance = tile_variance[0]
    coeffs = match_coeffs[0]
    count = images.shape[0]
    tile = images.shape[1]
    held_most = max(2, 2 * count // n_sky)
    positions = GRID * GRID
    per_dev = GRID // n_visit
    dest = tile_patch[0, :, 0]
    offsets = tile_offset[0]
    band_row = band_table(row_taps, tile)
    band_col = band_table(col_taps, tile)
    row_side = band_row.transpose(1, 0, 2).reshape(tile, BASIS * tile)
    col_side = band_col.transpose(2, 0, 1).reshape(tile, BASIS * tile)
    order = jnp.arange(count)
    earlier = (dest[:, None] == dest[None, :]) & (order[None, :] < order[:, None])
    rank = jnp.sum(earlier.astype(jnp.int32), axis=1)
    slot = dest * held_most + rank
    slots_all = n_sky * held_most
    pick = (jnp.arange(slots_all)[:, None] == slot[None, :]).astype(jnp.bfloat16)
    weight_src = 1.0 / jnp.mean(variance.astype(jnp.float32), axis=(1, 2))
    w_parts = split_exact(weight_src)
    meta_row = jnp.concatenate(
        [coeffs, (offsets + 1).astype(jnp.bfloat16)[:, None]]
        + [part[:, None] for part in w_parts]
        + [jnp.zeros((count, tile - BASIS - 4), jnp.bfloat16)],
        axis=1,
    )
    meta = jnp.concatenate(
        [meta_row[:, None, :], jnp.zeros((count, META - 1, tile), jnp.bfloat16)], axis=1
    )
    image_meta = jnp.concatenate([images, meta], axis=1)
    send_im = jnp.dot(
        pick, image_meta.reshape(count, (tile + META) * tile), preferred_element_type=jnp.float32
    )
    send_im = send_im.astype(jnp.bfloat16).reshape(n_sky, held_most, tile + META, tile)
    me = lax.axis_index("sky")
    shift = (dest - me) % n_sky
    pick_shift = (jnp.arange(slots_all)[:, None] == (shift * held_most + rank)[None, :])
    send_var = jnp.dot(
        pick_shift.astype(jnp.bfloat16), variance.reshape(count, tile * tile),
        preferred_element_type=jnp.float32,
    )
    send_var = send_var.astype(jnp.bfloat16).reshape(n_sky, held_most, tile, tile)

    part_im = lax.all_to_all(send_im, "sky", split_axis=0, concat_axis=0, tiled=True)
    part_im = part_im.reshape(slots_all, tile + META, tile)
    got_meta = part_im[:, tile, :].astype(jnp.float32)
    got_coef = got_meta[:, :BASIS]
    place = got_meta[:, BASIS].astype(jnp.int32) - 1
    valid = place >= 0
    weight = (got_meta[:, BASIS + 1] + got_meta[:, BASIS + 2]) + got_meta[:, BASIS + 3]
    weight = jnp.where(valid, weight, 0.0)
    tile_row = jnp.where(valid, place // GRID, -1)
    tile_col = place % GRID
    where = (tile_row, tile_col // per_dev, tile_col % per_dev)
    psf_part = jnp.sum(weight[:, None] * got_coef, axis=0)
    weight_part = jnp.sum(weight)
    weight_pos = jnp.sum(
        jnp.where(jnp.arange(positions)[:, None] == place[None, :], weight[None, :], 0.0), axis=1
    )
    pos_lanes = weight_pos.reshape(GRID, n_visit, per_dev).transpose(1, 2, 0)
    pos_lanes = jnp.concatenate(
        [pos_lanes, jnp.zeros((n_visit, per_dev, tile - GRID), jnp.float32)], axis=2
    ).reshape(n_visit, 1, per_dev * tile)
    psf_row = jnp.concatenate(
        [psf_part, weight_part[None], jnp.zeros((per_dev * tile - BASIS - 1,), jnp.float32)]
    )
    extra = jnp.concatenate(
        [
            pos_lanes,
            jnp.broadcast_to(psf_row[None, None, :], (n_visit, 1, per_dev * tile)),
            jnp.zeros((n_visit, EXTRA - 2, per_dev * tile), jnp.float32),
        ],
        axis=1,
    )
    image_pos = image_field(
        where, weight, got_coef.reshape(slots_all * BASIS), part_im, row_side, col_side, extra,
        (n_visit, GRID * tile + EXTRA, per_dev * tile),
    )
    image_share = lax.psum_scatter(image_pos, "visit", scatter_dimension=0, tiled=True)[0]

    got_var = [send_var[0]]
    for step in range(1, n_sky):
        pairs = [(src, (src + step) % n_sky) for src in range(n_sky)]
        got_var.append(lax.ppermute(send_var[step], "sky", perm=pairs))
    part_var = jnp.stack(got_var).reshape(slots_all, tile, tile)
    source = (me - jnp.arange(n_sky)) % n_sky

    def by_shift(values):
        return jnp.take(values.reshape(n_sky, held_most), source, axis=0).reshape(slots_all)

    var_where = tuple(by_shift(values) for values in where)
    var_pos = variance_field(
        var_where, by_shift(weight * weight), part_var, (n_visit, GRID * tile, per_dev * tile)
    )
    var_share = lax.psum_scatter(var_pos, "visit", scatter_dimension=0, tiled=True)[0]

    body_rows = GRID * tile
    pos_weight = image_share[body_rows, :].reshape(per_dev, tile)[:, :GRID]
    denom = jnp.maximum(pos_weight, weight_floor).T
    denom = jnp.broadcast_to(denom[:, None, :, None], (GRID, tile, per_dev, tile))
    denom = denom.reshape(body_rows, per_dev * tile)
    coadd_image = image_share[:body_rows, :] / denom
    coadd_variance = var_share / (denom * denom)

    psf_total = image_share[body_rows + 1, :BASIS]
    weight_total = image_share[body_rows + 1, BASIS]
    share = psf_total / weight_total
    high = lax.Precision.HIGHEST
    coadd_psf = jnp.einsum(
        "k,ka,kb->ab",
        share,
        col_taps.astype(jnp.float32),
        row_taps.astype(jnp.float32),
        precision=high,
    )[None]
    return (coadd_image, coadd_variance, coadd_psf)


def solution(mesh):
    return jax.shard_map(
        shards,
        mesh=mesh,
        in_specs=(
            P("visit", "sky", None, None),
            P("visit", "sky", None, None),
            P("visit", "sky", None),
            P("visit", "sky", None),
            P("visit", "sky"),
            P(),
            P(),
        ),
        out_specs=(P("sky", "visit"), P("sky", "visit"), P("sky", None, None)),
        check_vma=False,
    )
```

time: 232 us -> 228 us (0.983)
  waiting for transfers between devices: 158 us -> 121 us
  starting transfers between devices: 11.1 us -> 40.9 us
  other arithmetic: 11.6 us -> 14.1 us
    all_to_all x2 -> x1, waiting for transfers between devices: 97.7 us -> 50.1 us  [shards(): lax.all_to_all(send_im, 'sky', split_axis=0, concat_axis=0, tiled=True)]
    ppermute x0 -> x7, starting transfers between devices: none -> 33.4 us  [shards(): got_var.append(lax.ppermute(send_var[step], 'sky', perm=pairs))]
    ppermute x0 -> x7, waiting for transfers between devices: none -> 18.3 us  [shards(): got_var.append(lax.ppermute(send_var[step], 'sky', perm=pairs))]
    reduce_scatter x2, waiting for transfers between devices: 60.3 us -> 52.7 us  [the longest x1 52.6 us: shards(): lax.psum_scatter(var_pos, 'visit', scatter_dimension=0, tiled=True)[0]]
    all_to_all x2 -> x1, starting transfers between devices: 11 us -> 7.38 us  [shards(): lax.all_to_all(send_im, 'sky', split_axis=0, concat_axis=0, tiled=True)]
    div x0 -> x1, other arithmetic: none -> 3.26 us  [shards(): coadd_variance = var_share / (denom * denom)]
    unnamed x19 -> x22, local copies, waits for them, and re-layouts: 6.1 us -> 2.95 us
  transfers between devices with their start and end apart: 4 -> 10, of which waited for: 3 -> 5; matrix products, arithmetic and copies ran while one was open for 4% -> 6% of each run, Pallas kernels for 5% -> 2%
where the time goes in v2:
time: 228 us; the launch traced here: 227 us
  waiting for transfers between devices  121 us (53%)
  starting transfers between devices  40.9 us (18%)
  Pallas kernels  17.3 us (8%)
  local copies, waits for them, and re-layouts  16.1 us (7%)
  between operations  14.4 us (6%)
  other arithmetic  14.1 us (6%)
  matrix products  3.25 us (1%)
    reduce_scatter x1, waiting for transfers between devices, shards(): lax.psum_scatter(var_pos, 'visit', scatter_dimension=0, tiled=True)[0]  52.6 us
    all_to_all x1, waiting for transfers between devices, shards(): lax.all_to_all(send_im, 'sky', split_axis=0, concat_axis=0, tiled=True)  50.1 us
    ppermute x7, starting transfers between devices, shards(): got_var.append(lax.ppermute(send_var[step], 'sky', perm=pairs))  33.4 us
    ppermute x7, waiting for transfers between devices, shards(): got_var.append(lax.ppermute(send_var[step], 'sky', perm=pairs))  18.3 us
    pallas_call x1, Pallas kernels, image_field(): pl.pallas_call(image_kernel, out_shape=jax.ShapeDtypeStruct(field_shape,...  12.2 us
    all_to_all x1, starting transfers between devices, shards(): lax.all_to_all(send_im, 'sky', split_axis=0, concat_axis=0, tiled=True)  7.38 us
    pallas_call x1, Pallas kernels, variance_field(): pl.pallas_call(variance_kernel, out_shape=jax.ShapeDtypeStruct(field_shap...  5.04 us
  transfers between devices with their start and end apart: 10, of which 5 were waited for; matrix products, arithmetic and copies ran while one was open for 6% of the time, Pallas kernels for 2%

profile of v2, /device:TPU:0, one launch (start us, length us, event | category | flops | bytes accessed | tf_op | source)
XLA Modules:
  0.0 227.0 jit_solution(8296742152780127300)
XLA Ops:
  7.2 1.6 convert_reduce_fusion
  9.4 0.9 convert_reduce_fusion.1
  10.7 0.8 copy.50
  12.4 1.5 maximum_maximum_fusion
  13.9 0.8 fusion.2
  14.7 1.8 copy.56
  16.5 7.4 %all-to-all-start = ((bf16[8,8,144,128]{3,2,1,0:T(8,128)(2,1)}), bf16[8,8,144,128]{3,2,1,0:T(8,128)(2,1)S(1)}, u32[]{:S(2)}, u32[]{:S(2)}) async-start(bf16[8,8,144,128]{3,2,1,0:T(8,128)(2,1)} %copy.56), calls=%async_computation | async-start | bytes 4718592 | tf_op jit(solution)/shard_map/all_to_all | solution.py:168
  24.0 0.7 fusion.7
  24.8 0.9 copy.61.col_side_ref
  25.7 0.7 fusion.8
  26.7 0.9 copy.60.row_side_ref
  27.7 50.1 %all-to-all-done = bf16[8,8,144,128]{3,2,1,0:T(8,128)(2,1)S(1)} async-done(((bf16[8,8,144,128]{3,2,1,0:T(8,128)(2,1)}), bf16[8,8,144,128]{3,2,1,0:T(8,128)(2,1)S(1)}, u32[]{:S(2)}, u32[]{:S(2)}) %all-to-all-start) | async-done | bytes 2359328 | tf_op jit(solution)/shard_map/all_to_all | solution.py:168
  78.3 0.8 and_select_fusion.3
  79.8 0.7 reshape.288.coef_ref
  82.0 0.7 maximum_maximum_fusion.1.extra_ref
  82.7 12.2 %shard_map.94 = f32[4,1032,256]{2,1,0:T(8,128)} custom-call(s32[64]{0:T(128)} %get-tuple-element.43.row_ref, s32[64]{0:T(128)} %get-tuple-element.42.group_ref, s32[64]{0:T(128)} %get-tuple-element.17.sub_ref, f32[64]{0:T(128)} %copy-done.4, f32[576]{0:T(1024)} %reshape.288.coef_ref, bf16[64,144,128]{2,1,0:T(8,128)(2,1)} %bitcast.110, ...), custom_call_target="tpu_custom_call" | custom-call | flops 4831838208 | bytes 6586368 | tf_op jit(solution)/shard_map/pallas_call | solution.py:99
  95.0 1.1 copy-done.1
  96.1 0.8 convolution_convert_fusion.1
  97.1 13.3 %collective-permute-start = (bf16[8,128,128]{2,1,0:T(8,128)(2,1)S(1)}, bf16[8,128,128]{2,1,0:T(8,128)(2,1)S(1)}, u32[]{:S(2)}, u32[]{:S(2)}) collective-permute-start(bf16[8,128,128]{2,1,0:T(8,128)(2,1)S(1)} %copy.63), channel_id=1, source_target_pairs={{0,4},{4,8},{8,12},{12,16},{16,20},{20,24},{24,28},{28,0},{1,5},{5... | collective-permute-start | bytes 786440 | tf_op jit(solution)/shard_map/ppermute | solution.py:208
  110.5 5.2 %collective-permute-start.1 = (bf16[8,128,128]{2,1,0:T(8,128)(2,1)S(1)}, bf16[8,128,128]{2,1,0:T(8,128)(2,1)S(1)}, u32[]{:S(2)}, u32[]{:S(2)}) collective-permute-start(bf16[8,128,128]{2,1,0:T(8,128)(2,1)S(1)} %copy.64), channel_id=1, source_target_pairs={{0,8},{4,12},{8,16},{12,20},{16,24},{20,28},{24,0},{28,4},{1,9},{5... | collective-permute-start | bytes 786440 | tf_op jit(solution)/shard_map/ppermute | solution.py:208
  115.8 5.3 %collective-permute-start.3 = (bf16[8,128,128]{2,1,0:T(8,128)(2,1)S(1)}, bf16[8,128,128]{2,1,0:T(8,128)(2,1)S(1)}, u32[]{:S(2)}, u32[]{:S(2)}) collective-permute-start(bf16[8,128,128]{2,1,0:T(8,128)(2,1)S(1)} %copy.66), channel_id=1, source_target_pairs={{0,16},{4,20},{8,24},{12,28},{16,0},{20,4},{24,8},{28,12},{1,17},{... | collective-permute-start | bytes 786440 | tf_op jit(solution)/shard_map/ppermute | solution.py:208
  121.4 2.4 %collective-permute-start.5 = (bf16[8,128,128]{2,1,0:T(8,128)(2,1)S(1)}, bf16[8,128,128]{2,1,0:T(8,128)(2,1)S(1)}, u32[]{:S(2)}, u32[]{:S(2)}) collective-permute-start(bf16[8,128,128]{2,1,0:T(8,128)(2,1)S(1)} %copy.68), channel_id=1, source_target_pairs={{0,24},{4,28},{8,0},{12,4},{16,8},{20,12},{24,16},{28,20},{1,25},{... | collective-permute-start | bytes 786440 | tf_op jit(solution)/shard_map/ppermute | solution.py:208
  123.9 7.1 %collective-permute-start.6 = (bf16[8,128,128]{2,1,0:T(8,128)(2,1)S(1)}, bf16[8,128,128]{2,1,0:T(8,128)(2,1)S(1)}, u32[]{:S(2)}, u32[]{:S(2)}) collective-permute-start(bf16[8,128,128]{2,1,0:T(8,128)(2,1)S(1)} %copy.69), channel_id=1, source_target_pairs={{0,28},{4,0},{8,4},{12,8},{16,12},{20,16},{24,20},{28,24},{1,29},{... | collective-permute-start | bytes 786440 | tf_op jit(solution)/shard_map/ppermute | solution.py:208
  131.0 12.3 %collective-permute-done.2 = bf16[8,128,128]{2,1,0:T(8,128)(2,1)S(1)} collective-permute-done((bf16[8,128,128]{2,1,0:T(8,128)(2,1)S(1)}, bf16[8,128,128]{2,1,0:T(8,128)(2,1)S(1)}, u32[]{:S(2)}, u32[]{:S(2)}) %collective-permute-start.2) | collective-permute-done | bytes 262176 | tf_op jit(solution)/shard_map/ppermute | solution.py:208
  143.4 1.4 collective-permute-done.5
  144.9 4.6 %collective-permute-done.6 = bf16[8,128,128]{2,1,0:T(8,128)(2,1)S(1)} collective-permute-done((bf16[8,128,128]{2,1,0:T(8,128)(2,1)S(1)}, bf16[8,128,128]{2,1,0:T(8,128)(2,1)S(1)}, u32[]{:S(2)}, u32[]{:S(2)}) %collective-permute-start.6) | collective-permute-done | bytes 262176 | tf_op jit(solution)/shard_map/ppermute | solution.py:208
  154.5 5.0 %shard_map.95 = f32[4,1024,256]{2,1,0:T(8,128)} custom-call(s32[64]{0:T(128)} %reshape.294.row_ref, s32[64]{0:T(128)} %reshape.295.group_ref, s32[64]{0:T(128)} %reshape.296.sub_ref, f32[64]{0:T(128)} %select_n.124.w2_ref, bf16[64,128,128]{2,1,0:T(8,128)(2,1)} %bitcast.108), custom_call_target="tpu_custom_call" | custom-call | tf_op jit(solution)/shard_map/pallas_call | solution.py:90
  159.6 1.3 slice.117
  160.9 0.7 slice.107
  161.7 1.3 fusion.35
  163.9 52.6 %reduce-scatter.5.cloned.1.call-done = f32[1,1024,256]{2,1,0:T(8,128)} async-done(((f32[4,1024,256]{2,1,0:T(8,128)}), f32[1,1024,256]{2,1,0:T(8,128)}) %reduce-scatter.5.cloned.1.call-update) | async-done | bytes 1048592 | tf_op jit(solution)/shard_map/reduce_scatter | solution.py:219
  216.9 3.3 %fusion.13 = (f32[1024,256]{1,0:T(8,128)}, f32[1024,256]{1,0:T(8,128)}) fusion(f32[1,1024,256]{2,1,0:T(8,128)} %reduce-scatter.5.cloned.1.call-done, f32[128,8,2,128]{3,2,1,0:T(2,128)S(1)} %bitcast.106, f32[1,1032,256]{2,1,0:T(8,128)} %reduce-scatter.3.cloned.1.call-done), kind=kLoop, calls=%fused_computation.25 | loop fusion | flops 786432 | bytes 5242880 | tf_op jit(solution)/shard_map/div | solution.py:227
  (93 shorter events, 12.4 us)
Async XLA Ops:
  7.2 18.5 %copy-start = (bf16[9,41]{1,0:T(8,128)(2,1)S(1)}, bf16[9,41]{1,0:T(8,128)(2,1)}, u32[]{:S(2)}) copy-start(bf16[9,41]{1,0:T(8,128)(2,1)} %param.14) | copy-start | bytes 2218
  16.5 7.5 %copy-start.5 = (bf16[9,41]{1,0:T(8,128)(2,1)S(1)}, bf16[9,41]{1,0:T(8,128)(2,1)}, u32[]{:S(2)}) copy-start(bf16[9,41]{1,0:T(8,128)(2,1)} %param.15) | copy-start | bytes 2218
  16.5 61.2 %all-to-all-start = ((bf16[8,8,144,128]{3,2,1,0:T(8,128)(2,1)}), bf16[8,8,144,128]{3,2,1,0:T(8,128)(2,1)S(1)}, u32[]{:S(2)}, u32[]{:S(2)}) async-start(bf16[8,8,144,128]{3,2,1,0:T(8,128)(2,1)} %copy.56), calls=%async_computation | async-start | bytes 4718592 | tf_op jit(solution)/shard_map/all_to_all | solution.py:168
  23.9 135.7 %reduce-scatter.3.cloned.1.call-start = ((), (), s32[]{:S(2)}) async-start(), calls=%async_computation.3 | async-start | bytes 5283840 | tf_op jit(solution)/shard_map/reduce_scatter | solution.py:203
  77.8 4.9 %copy-start.3 = (bf16[8,8,144,128]{3,2,1,0:T(8,128)(2,1)}, bf16[8,8,144,128]{3,2,1,0:T(8,128)(2,1)S(1)}, u32[]{:S(2)}) copy-start(bf16[8,8,144,128]{3,2,1,0:T(8,128)(2,1)S(1)} %all-to-all-done) | copy-start | bytes 7077892
  79.7 3.0 %copy-start.4 = (f32[64]{0:T(128)}, f32[64]{0:T(128)S(1)}, u32[]{:S(2)}) copy-start(f32[64]{0:T(128)S(1)} %get-tuple-element.16.w_ref) | copy-start | bytes 772
  94.9 1.2 copy-start.1
  94.9 121.6 %reduce-scatter.5.cloned.1.call-start = ((), (), s32[]{:S(2)}) async-start(), calls=%async_computation.4 | async-start | bytes 5242880 | tf_op jit(solution)/shard_map/reduce_scatter | solution.py:219
  97.1 24.3 %collective-permute-start = (bf16[8,128,128]{2,1,0:T(8,128)(2,1)S(1)}, bf16[8,128,128]{2,1,0:T(8,128)(2,1)S(1)}, u32[]{:S(2)}, u32[]{:S(2)}) collective-permute-start(bf16[8,128,128]{2,1,0:T(8,128)(2,1)S(1)} %copy.63), channel_id=1, source_target_pairs={{0,4},{4,8},{8,12},{12,16},{16,20},{20,24},{24,28},{28,0},{1,5},{5... | collective-permute-start | bytes 786440 | tf_op jit(solution)/shard_map/ppermute | solution.py:208
  110.5 13.4 %collective-permute-start.1 = (bf16[8,128,128]{2,1,0:T(8,128)(2,1)S(1)}, bf16[8,128,128]{2,1,0:T(8,128)(2,1)S(1)}, u32[]{:S(2)}, u32[]{:S(2)}) collective-permute-start(bf16[8,128,128]{2,1,0:T(8,128)(2,1)S(1)} %copy.64), channel_id=1, source_target_pairs={{0,8},{4,12},{8,16},{12,20},{16,24},{20,28},{24,0},{28,4},{1,9},{5... | collective-permute-start | bytes 786440 | tf_op jit(solution)/shard_map/ppermute | solution.py:208
  115.7 27.6 %collective-permute-start.2 = (bf16[8,128,128]{2,1,0:T(8,128)(2,1)S(1)}, bf16[8,128,128]{2,1,0:T(8,128)(2,1)S(1)}, u32[]{:S(2)}, u32[]{:S(2)}) collective-permute-start(bf16[8,128,128]{2,1,0:T(8,128)(2,1)S(1)} %copy.65), channel_id=1, source_target_pairs={{0,12},{4,16},{8,20},{12,24},{16,28},{20,0},{24,4},{28,8},{1,13},{... | collective-permute-start | bytes 786440 | tf_op jit(solution)/shard_map/ppermute | solution.py:208
  115.8 27.5 %collective-permute-start.3 = (bf16[8,128,128]{2,1,0:T(8,128)(2,1)S(1)}, bf16[8,128,128]{2,1,0:T(8,128)(2,1)S(1)}, u32[]{:S(2)}, u32[]{:S(2)}) collective-permute-start(bf16[8,128,128]{2,1,0:T(8,128)(2,1)S(1)} %copy.66), channel_id=1, source_target_pairs={{0,16},{4,20},{8,24},{12,28},{16,0},{20,4},{24,8},{28,12},{1,17},{... | collective-permute-start | bytes 786440 | tf_op jit(solution)/shard_map/ppermute | solution.py:208
  121.2 22.2 %collective-permute-start.4 = (bf16[8,128,128]{2,1,0:T(8,128)(2,1)S(1)}, bf16[8,128,128]{2,1,0:T(8,128)(2,1)S(1)}, u32[]{:S(2)}, u32[]{:S(2)}) collective-permute-start(bf16[8,128,128]{2,1,0:T(8,128)(2,1)S(1)} %copy.67), channel_id=1, source_target_pairs={{0,20},{4,24},{8,28},{12,0},{16,4},{20,8},{24,12},{28,16},{1,21},{... | collective-permute-start | bytes 786440 | tf_op jit(solution)/shard_map/ppermute | solution.py:208
  121.4 23.4 %collective-permute-start.5 = (bf16[8,128,128]{2,1,0:T(8,128)(2,1)S(1)}, bf16[8,128,128]{2,1,0:T(8,128)(2,1)S(1)}, u32[]{:S(2)}, u32[]{:S(2)}) collective-permute-start(bf16[8,128,128]{2,1,0:T(8,128)(2,1)S(1)} %copy.68), channel_id=1, source_target_pairs={{0,24},{4,28},{8,0},{12,4},{16,8},{20,12},{24,16},{28,20},{1,25},{... | collective-permute-start | bytes 786440 | tf_op jit(solution)/shard_map/ppermute | solution.py:208
  123.9 25.6 %collective-permute-start.6 = (bf16[8,128,128]{2,1,0:T(8,128)(2,1)S(1)}, bf16[8,128,128]{2,1,0:T(8,128)(2,1)S(1)}, u32[]{:S(2)}, u32[]{:S(2)}) collective-permute-start(bf16[8,128,128]{2,1,0:T(8,128)(2,1)S(1)} %copy.69), channel_id=1, source_target_pairs={{0,28},{4,0},{8,4},{12,8},{16,12},{20,16},{24,20},{28,24},{1,29},{... | collective-permute-start | bytes 786440 | tf_op jit(solution)/shard_map/ppermute | solution.py:208
  149.5 5.0 %copy-start.2 = (bf16[8,8,128,128]{3,2,1,0:T(8,128)(2,1)}, bf16[8,8,128,128]{3,2,1,0:T(8,128)(2,1)S(1)}, u32[]{:S(2)}) copy-start(bf16[8,8,128,128]{3,2,1,0:T(8,128)(2,1)S(1)} %bitcast_dynamic-update-slice_fusion) | copy-start | bytes 6291460
Sparse Core Ops, SparseCore 0:
  95.0 59.7 reduce-scatter.2
  159.7 56.8 reduce-scatter.4
